TPU v7x, 32 devices: a whole 2x2x4 slice. The times are simulated.
32 devices in a mesh: videos: 2 (over y), ha: 4 (over z), wa: 2 (over x), ta: 2 (over core).
Axes of the slice: x: 2, y: 2, z: 4, core: 2. Of those that a mesh axis runs over, the one named last changes fastest.
Arguments:
- latents: bfloat16 [12, 8, 64, 512], P(('videos', 'ta'), 'ha', 'wa'), parts along dimension 0, may hold values from -200 to 200
- norm1_gain: float32 [512], replicated, may hold values from 0.25 to 1.75
- norm1_shift: float32 [512], replicated, may hold values from -2.5 to 2.5
- up_weight: bfloat16 [3, 3, 512, 256], replicated, may hold values from -0.1875 to 0.1875
- norm2_gain: float32 [256], replicated, may hold values from 0.25 to 1.75
- norm2_shift: float32 [256], replicated, may hold values from -2.5 to 2.5
- conv_a: bfloat16 [3, 3, 3, 256, 256], replicated, may hold values from -0.078125 to 0.078125
- norm3_gain: float32 [256], replicated, may hold values from 0.25 to 1.75
- norm3_shift: float32 [256], replicated, may hold values from -2.5 to 2.5
- conv_b: bfloat16 [3, 3, 3, 256, 256], replicated, may hold values from -0.078125 to 0.078125
Outputs:
- decoded: bfloat16 [12, 16, 128, 256], P(('videos', 'ta'), 'ha', 'wa'), parts along dimension 0
There are 2 independent parts, one for each index of `videos`. A program takes and returns all parts, laid end to end along the dimension named above; an argument that names none is the same for every part. Nothing has to cross between parts.
All inputs are finite; a program needn't handle non-finite values.
Results may differ from a plain program's by a relative error of at most 0.008.
Values may be sent and summed in bfloat16 or wider, within the bound.
No kernel may reach another device: no remote copies, remote signals or barrier semaphores. Data moves between devices by JAX's collectives and lax.ppermute only.
A program may use at most 64 MiB of HBM per device.

v0:
```python
import jax
import jax.numpy as jnp
from jax import lax
from jax.sharding import PartitionSpec as P

GROUPS = 32
EPSILON = 1e-06


def passed_along(block, axis, distance):
    devices = range(lax.axis_size(axis))
    route = [(i - distance, i) for i in devices if i - distance in devices]
    return lax.ppermute(block, axis, route)


def padded_2(x, sides, width):
    for axis, dim in sides:
        size, length = (lax.axis_size(axis), x.shape[dim])
        up = [(i, (i + 1) % size) for i in range(size - 1)]
        down = [(j, i) for i, j in up]
        last = lax.slice_in_dim(x, length - width, length, axis=dim)
        initial = lax.slice_in_dim(x, 0, width, axis=dim)
        before = lax.ppermute(last, axis, up)
        after = lax.ppermute(initial, axis, down)
        x = jnp.concatenate([before, x, after], axis=dim)
    return x


def activate(values, sample, scale_vec, shift_vec):
    channels = values.shape[-1]
    group_width = channels // GROUPS
    grouped = sample.reshape(-1, GROUPS, group_width)
    entries = (
        grouped.shape[0]
        * group_width
        * lax.axis_size("ha")
        * lax.axis_size("wa")
        * lax.axis_size("ta")
    )
    totals, squares = lax.psum(
        (jnp.sum(grouped, axis=(0, 2)), jnp.sum(grouped * grouped, axis=(0, 2))), ("ha", "wa", "ta")
    )
    average = totals / entries
    spread = squares / entries - average * average
    scaling = lax.rsqrt(spread + EPSILON)
    normed = (values - jnp.repeat(average, group_width)) * jnp.repeat(
        scaling, group_width
    ) * scale_vec + shift_vec
    return jax.nn.silu(normed).astype(jnp.bfloat16)


def parity_merge(lead_part, mid_part, tail_part, axis_pos):
    pad_end = [(0, 0)] * lead_part.ndim
    pad_front = [(0, 0)] * lead_part.ndim
    pad_end[axis_pos] = (0, 1)
    pad_front[axis_pos] = (1, 0)
    even_part = jnp.pad(lead_part, pad_end) + jnp.pad(tail_part, pad_front)
    odd_part = jnp.pad(mid_part, pad_end)
    stacked = jnp.stack([even_part, odd_part], axis=axis_pos + 1)
    new_shape = list(even_part.shape)
    new_shape[axis_pos] = new_shape[axis_pos] * 2
    return stacked.reshape(new_shape)


def spread_taps(source, kernel):
    frames, height, across, channels = source.shape
    flattened = source.reshape(-1, channels)
    products = [
        [
            jnp.dot(flattened, kernel[tap_y, tap_x], preferred_element_type=jnp.float32).reshape(
                frames, height, across, -1
            )
            for tap_x in range(3)
        ]
        for tap_y in range(3)
    ]
    columns = [
        parity_merge(products[0][tap_x], products[1][tap_x], products[2][tap_x], 1)
        for tap_x in range(3)
    ]
    return parity_merge(columns[0], columns[1], columns[2], 2)


def valid_conv(padded, kernel, frames, height, across):
    result = jnp.zeros((frames * height * across, kernel.shape[-1]), jnp.float32)
    for step_t in range(3):
        for step_y in range(3):
            for step_x in range(3):
                window = padded[
                    step_t : step_t + frames, step_y : step_y + height, step_x : step_x + across
                ]
                result = result + jnp.dot(
                    window.reshape(-1, window.shape[-1]),
                    kernel[step_t, step_y, step_x],
                    preferred_element_type=jnp.float32,
                )
    return result.reshape(frames, height, across, -1)


def causal_extend(values):
    earlier = passed_along(values[-2:], "ta", 1)
    opening = jnp.concatenate([values[:1], values[:1]], axis=0)
    earlier = jnp.where(lax.axis_index("ta") == 0, opening, earlier)
    return jnp.concatenate([earlier, values], axis=0)


def bordered_one(values):
    return padded_2(values, (("ha", 1), ("wa", 2)), 1)


def per_device(
    latents,
    norm1_gain,
    norm1_shift,
    up_weight,
    norm2_gain,
    norm2_shift,
    conv_a,
    norm3_gain,
    norm3_shift,
    conv_b,
):
    frames, height, across, channels = latents.shape
    latent_f = latents.astype(jnp.float32)
    activated = activate(latent_f, latent_f, norm1_gain, norm1_shift)
    spilled = spread_taps(activated, up_weight)
    from_below = passed_along(spilled[:, 0], "ha", -1)
    row_fixed = spilled[:, 1 : 2 * height + 1]
    row_fixed = jnp.concatenate(
        [row_fixed[:, :-1], row_fixed[:, -1:] + from_below[:, None]], axis=1
    )
    beside = passed_along(row_fixed[:, :, 0], "wa", -1)
    lifted = jnp.concatenate(
        [
            row_fixed[:, :, 1 : 2 * across],
            row_fixed[:, :, 2 * across : 2 * across + 1] + beside[:, :, None],
        ],
        axis=2,
    )
    lifted = lifted.astype(jnp.bfloat16)
    lifted_f = lifted.astype(jnp.float32)
    first_act = activate(lifted_f, lifted_f, norm2_gain, norm2_shift)
    out_h = 2 * height
    out_w = 2 * across
    hidden = valid_conv(
        bordered_one(causal_extend(first_act)), conv_a, frames, out_h, out_w
    ).astype(jnp.bfloat16)
    hidden_f = hidden.astype(jnp.float32)
    second_act = activate(hidden_f, hidden_f, norm3_gain, norm3_shift)
    framed = bordered_one(causal_extend(second_act))
    branch = valid_conv(framed, conv_b, frames, out_h, out_w)
    return (lifted_f + branch).astype(jnp.bfloat16)


def solution(mesh):
    return jax.shard_map(
        per_device,
        mesh=mesh,
        in_specs=(
            P(("videos", "ta"), "ha", "wa", None),
            P(),
            P(),
            P(),
            P(),
            P(),
            P(),
            P(),
            P(),
            P(),
        ),
        out_specs=P(("videos", "ta"), "ha", "wa", None),
        check_vma=False,
    )
```

profile of v0, /device:TPU:0, one launch (start us, length us, event | category | flops | bytes accessed | tf_op | source)
XLA Modules:
  0.0 204.1 jit_solution(1638593344820532898)
XLA Ops:
  1.4 34.9 %all-reduce.14 = (f32[32]{0:T(128)S(1)}, f32[32]{0:T(128)S(1)}) all-reduce(f32[32]{0:T(128)S(1)} %reduce_sum.77, f32[32]{0:T(128)S(1)} %reduce_sum.74), channel_id=1, replica_groups=mesh['videos'=2,'ha'=4,'wa'=2,'ta'=2] {'ha','wa','ta'}, use_global_device_ids=true, to_apply=%region_5.6 | all-reduce | flops 64 | bytes 512 | tf_op jit(solution)/shard_map/psum | solution.py:40
  50.9 1.3 collective-permute-start
  52.6 6.2 %collective-permute-done = f32[3,66,256]{2,1,0:T(8,128)S(1)} collective-permute-done((f32[3,66,256]{2,1,0:T(8,128)S(1)}, f32[3,66,256]{2,1,0:T(8,128)S(1)}, u32[]{:S(2)}, u32[]{:S(2)}) %collective-permute-start) | collective-permute-done | bytes 202784 | tf_op jit(solution)/shard_map/ppermute | solution.py:13
  59.0 1.3 collective-permute-start.1
  60.7 3.9 %collective-permute-done.1 = f32[3,4,256]{2,1,0:T(4,128)S(1)} collective-permute-done((f32[3,4,256]{2,1,0:T(4,128)S(1)}, f32[3,4,256]{2,1,0:T(4,128)S(1)}, u32[]{:S(2)}, u32[]{:S(2)}) %collective-permute-start.1) | collective-permute-done | bytes 12320 | tf_op jit(solution)/shard_map/ppermute | solution.py:13
  65.5 29.5 %all-reduce.13 = (f32[32]{0:T(128)S(1)}, f32[32]{0:T(128)S(1)}) all-reduce(f32[32]{0:T(128)S(1)} %reduce_sum.89, f32[32]{0:T(128)S(1)} %reduce_sum.83), channel_id=1, replica_groups=mesh['videos'=2,'ha'=4,'wa'=2,'ta'=2] {'ha','wa','ta'}, use_global_device_ids=true, to_apply=%region_11.12 | all-reduce | flops 64 | bytes 512 | tf_op jit(solution)/shard_map/psum | solution.py:40
  96.0 1.8 collective-permute-start.2
  100.0 1.3 collective-permute-start.4
  101.3 4.6 %collective-permute-start.3 = (bf16[5,1,64,256]{3,1,2,0:T(2,128)(2,1)S(1)}, bf16[5,1,64,256]{3,1,2,0:T(2,128)(2,1)S(1)}, u32[]{:S(2)}, u32[]{:S(2)}) collective-permute-start(bf16[5,1,64,256]{3,1,2,0:T(2,128)(2,1)S(1)} %get-tuple-element.81), channel_id=1, source_target_pairs={{0,4},{4,8},{8,12},{1,5},{5,9},{9,13},{2,6},{6,10},{10,14},{3,7},{... | collective-permute-start | bytes 491528 | tf_op jit(solution)/shard_map/ppermute | solution.py:23
  105.9 5.9 %collective-permute-done.4 = bf16[5,1,64,256]{3,1,2,0:T(2,128)(2,1)S(1)} collective-permute-done((bf16[5,1,64,256]{3,1,2,0:T(2,128)(2,1)S(1)}, bf16[5,1,64,256]{3,1,2,0:T(2,128)(2,1)S(1)}, u32[]{:S(2)}, u32[]{:S(2)}) %collective-permute-start.4) | collective-permute-done | bytes 163872 | tf_op jit(solution)/shard_map/ppermute | solution.py:24
  114.4 1.5 collective-permute-start.6
  117.2 1.7 pad_maximum_fusion.15
  120.1 2.3 %maximum_maximum_fusion = (bf16[5,6,65,256]{3,1,2,0:T(8,128)(2,1)S(1)}, bf16[5,6,65,256]{3,1,2,0:T(8,128)(2,1)S(1)}) fusion(bf16[5,1,64,256]{3,1,2,0:T(2,128)(2,1)S(1)} %collective-permute-done.4, bf16[3,4,64,256]{3,1,2,0:T(4,128)(2,1)S(1)} %fusion.13, bf16[2,4,64,256]{3,1,2,0:T(4,128)(2,1)S(1)} %maximum_select_fusion, ...), kind=kLoop, calls=%fused_computation.5 | loop fusion | flops 9984000 | bytes 3010560 | tf_op jit(solution)/shard_map/concatenate | solution.py:25
  122.4 1.6 fusion.182
  124.0 1.3 fusion.183
  133.7 30.7 %all-reduce.12 = (f32[32]{0:T(128)S(1)}, f32[32]{0:T(128)S(1)}) all-reduce(f32[32]{0:T(128)S(1)} %reduce_sum.113, f32[32]{0:T(128)S(1)} %reduce_sum.110), channel_id=1, replica_groups=mesh['videos'=2,'ha'=4,'wa'=2,'ta'=2] {'ha','wa','ta'}, use_global_device_ids=true, to_apply=%region_17.18 | all-reduce | flops 64 | bytes 512 | tf_op jit(solution)/shard_map/psum | solution.py:40
  165.6 1.8 collective-permute-start.7
  169.4 1.3 collective-permute-start.9
  170.7 4.6 %collective-permute-start.8 = (bf16[5,1,64,256]{3,1,2,0:T(2,128)(2,1)S(1)}, bf16[5,1,64,256]{3,1,2,0:T(2,128)(2,1)S(1)}, u32[]{:S(2)}, u32[]{:S(2)}) collective-permute-start(bf16[5,1,64,256]{3,1,2,0:T(2,128)(2,1)S(1)} %get-tuple-element.77), channel_id=1, source_target_pairs={{0,4},{4,8},{8,12},{1,5},{5,9},{9,13},{2,6},{6,10},{10,14},{3,7},{... | collective-permute-start | bytes 491528 | tf_op jit(solution)/shard_map/ppermute | solution.py:23
  175.3 6.0 %collective-permute-done.9 = bf16[5,1,64,256]{3,1,2,0:T(2,128)(2,1)S(1)} collective-permute-done((bf16[5,1,64,256]{3,1,2,0:T(2,128)(2,1)S(1)}, bf16[5,1,64,256]{3,1,2,0:T(2,128)(2,1)S(1)}, u32[]{:S(2)}, u32[]{:S(2)}) %collective-permute-start.9) | collective-permute-done | bytes 163872 | tf_op jit(solution)/shard_map/ppermute | solution.py:24
  183.8 1.3 collective-permute-start.11
  186.4 1.7 pad_maximum_fusion.6
  189.5 2.3 %maximum_maximum_fusion.1 = (bf16[5,6,65,256]{3,1,2,0:T(8,128)(2,1)S(1)}, bf16[5,6,65,256]{3,1,2,0:T(8,128)(2,1)S(1)}) fusion(bf16[5,1,64,256]{3,1,2,0:T(2,128)(2,1)S(1)} %collective-permute-done.9, bf16[3,4,64,256]{3,1,2,0:T(4,128)(2,1)S(1)} %fusion.14, bf16[2,4,64,256]{3,1,2,0:T(4,128)(2,1)S(1)} %maximum_select_fusion.1, ...), kind=kLoop, calls=%fused_computation.7 | loop fusion | flops 9984000 | bytes 3010560 | tf_op jit(solution)/shard_map/concatenate | solution.py:25
  191.8 1.6 fusion.180
  (205 shorter events, 52.3 us)
Async XLA Ops:
  50.9 44.4 %copy-start.2 = (f32[256]{0:T(256)S(1)}, f32[256]{0:T(256)}, u32[]{:S(2)}) copy-start(f32[256]{0:T(256)} %param.15) | copy-start | bytes 3076
  50.9 44.4 %copy-start.3 = (f32[256]{0:T(256)S(1)}, f32[256]{0:T(256)}, u32[]{:S(2)}) copy-start(f32[256]{0:T(256)} %param.14) | copy-start | bytes 3076
  50.9 7.8 %collective-permute-start = (f32[3,66,256]{2,1,0:T(8,128)S(1)}, f32[3,66,256]{2,1,0:T(8,128)S(1)}, u32[]{:S(2)}, u32[]{:S(2)}) collective-permute-start(f32[3,66,256]{2,1,0:T(8,128)S(1)} %get-tuple-element.53), channel_id=1, source_target_pairs={{4,0},{8,4},{12,8},{5,1},{9,5},{13,9},{6,2},{10,6},{14,10},{7,3},{... | collective-permute-start | bytes 608264 | tf_op jit(solution)/shard_map/ppermute | solution.py:13
  59.0 5.6 %collective-permute-start.1 = (f32[3,4,256]{2,1,0:T(4,128)S(1)}, f32[3,4,256]{2,1,0:T(4,128)S(1)}, u32[]{:S(2)}, u32[]{:S(2)}) collective-permute-start(f32[3,4,256]{2,1,0:T(4,128)S(1)} %fusion.176), channel_id=1, source_target_pairs={{2,0},{3,1},{6,4},{7,5},{10,8},{11,9},{14,12},{15,13},{18,16},{19,... | collective-permute-start | bytes 36872 | tf_op jit(solution)/shard_map/ppermute | solution.py:13
  96.0 2.9 %collective-permute-start.2 = (bf16[2,4,64,256]{3,1,2,0:T(4,128)(2,1)S(1)}, bf16[2,4,64,256]{3,1,2,0:T(4,128)(2,1)S(1)}, u32[]{:S(2)}, u32[]{:S(2)}) collective-permute-start(bf16[2,4,64,256]{3,1,2,0:T(4,128)(2,1)S(1)} %slice.594), channel_id=1, source_target_pairs={{0,1},{2,3},{4,5},{6,7},{8,9},{10,11},{12,13},{14,15},{16,17},{18,... | collective-permute-start | bytes 786440 | tf_op jit(solution)/shard_map/ppermute | solution.py:13
  97.9 19.0 %copy-start = (bf16[3,3,3,256,256]{4,3,2,1,0:T(8,128)(2,1)S(1)}, bf16[3,3,3,256,256]{4,3,2,1,0:T(8,128)(2,1)}, u32[]{:S(2)}) copy-start(bf16[3,3,3,256,256]{4,3,2,1,0:T(8,128)(2,1)} %param.16) | copy-start | bytes 10616836
  100.0 11.9 %collective-permute-start.4 = (bf16[5,1,64,256]{3,1,2,0:T(2,128)(2,1)S(1)}, bf16[5,1,64,256]{3,1,2,0:T(2,128)(2,1)S(1)}, u32[]{:S(2)}, u32[]{:S(2)}) collective-permute-start(bf16[5,1,64,256]{3,1,2,0:T(2,128)(2,1)S(1)} %get-tuple-element.82), channel_id=1, source_target_pairs={{4,0},{8,4},{12,8},{5,1},{9,5},{13,9},{6,2},{10,6},{14,10},{7,3},{... | collective-permute-start | bytes 491528 | tf_op jit(solution)/shard_map/ppermute | solution.py:24
  101.3 11.8 %collective-permute-start.3 = (bf16[5,1,64,256]{3,1,2,0:T(2,128)(2,1)S(1)}, bf16[5,1,64,256]{3,1,2,0:T(2,128)(2,1)S(1)}, u32[]{:S(2)}, u32[]{:S(2)}) collective-permute-start(bf16[5,1,64,256]{3,1,2,0:T(2,128)(2,1)S(1)} %get-tuple-element.81), channel_id=1, source_target_pairs={{0,4},{4,8},{8,12},{1,5},{5,9},{9,13},{2,6},{6,10},{10,14},{3,7},{... | collective-permute-start | bytes 491528 | tf_op jit(solution)/shard_map/ppermute | solution.py:23
  113.1 6.2 %collective-permute-start.5 = (bf16[5,6,1,256]{3,1,2,0:T(8,128)(2,1)S(1)}, bf16[5,6,1,256]{3,1,2,0:T(8,128)(2,1)S(1)}, u32[]{:S(2)}, u32[]{:S(2)}) collective-permute-start(bf16[5,6,1,256]{3,1,2,0:T(8,128)(2,1)S(1)} %get-tuple-element.61), channel_id=1, source_target_pairs={{0,2},{1,3},{4,6},{5,7},{8,10},{9,11},{12,14},{13,15},{16,18},{17,... | collective-permute-start | bytes 46088 | tf_op jit(solution)/shard_map/ppermute | solution.py:23
  114.4 5.7 %collective-permute-start.6 = (bf16[5,6,1,256]{3,1,2,0:T(8,128)(2,1)S(1)}, bf16[5,6,1,256]{3,1,2,0:T(8,128)(2,1)S(1)}, u32[]{:S(2)}, u32[]{:S(2)}) collective-permute-start(bf16[5,6,1,256]{3,1,2,0:T(8,128)(2,1)S(1)} %get-tuple-element.62), channel_id=1, source_target_pairs={{2,0},{3,1},{6,4},{7,5},{10,8},{11,9},{14,12},{15,13},{18,16},{19,... | collective-permute-start | bytes 46088 | tf_op jit(solution)/shard_map/ppermute | solution.py:24
  132.4 32.4 %copy-start.4 = (f32[256]{0:T(256)S(1)}, f32[256]{0:T(256)}, u32[]{:S(2)}) copy-start(f32[256]{0:T(256)} %param.18) | copy-start | bytes 3076
  132.4 32.4 %copy-start.5 = (f32[256]{0:T(256)S(1)}, f32[256]{0:T(256)}, u32[]{:S(2)}) copy-start(f32[256]{0:T(256)} %param.17) | copy-start | bytes 3076
  165.5 20.6 %copy-start.1 = (bf16[3,3,3,256,256]{4,3,2,1,0:T(8,128)(2,1)S(1)}, bf16[3,3,3,256,256]{4,3,2,1,0:T(8,128)(2,1)}, u32[]{:S(2)}) copy-start(bf16[3,3,3,256,256]{4,3,2,1,0:T(8,128)(2,1)} %param.19) | copy-start | bytes 10616836
  165.6 2.7 %collective-permute-start.7 = (bf16[2,4,64,256]{3,1,2,0:T(4,128)(2,1)S(1)}, bf16[2,4,64,256]{3,1,2,0:T(4,128)(2,1)S(1)}, u32[]{:S(2)}, u32[]{:S(2)}) collective-permute-start(bf16[2,4,64,256]{3,1,2,0:T(4,128)(2,1)S(1)} %slice.620), channel_id=1, source_target_pairs={{0,1},{2,3},{4,5},{6,7},{8,9},{10,11},{12,13},{14,15},{16,17},{18,... | collective-permute-start | bytes 786440 | tf_op jit(solution)/shard_map/ppermute | solution.py:13
  169.4 11.9 %collective-permute-start.9 = (bf16[5,1,64,256]{3,1,2,0:T(2,128)(2,1)S(1)}, bf16[5,1,64,256]{3,1,2,0:T(2,128)(2,1)S(1)}, u32[]{:S(2)}, u32[]{:S(2)}) collective-permute-start(bf16[5,1,64,256]{3,1,2,0:T(2,128)(2,1)S(1)} %get-tuple-element.78), channel_id=1, source_target_pairs={{4,0},{8,4},{12,8},{5,1},{9,5},{13,9},{6,2},{10,6},{14,10},{7,3},{... | collective-permute-start | bytes 491528 | tf_op jit(solution)/shard_map/ppermute | solution.py:24
  170.7 11.8 %collective-permute-start.8 = (bf16[5,1,64,256]{3,1,2,0:T(2,128)(2,1)S(1)}, bf16[5,1,64,256]{3,1,2,0:T(2,128)(2,1)S(1)}, u32[]{:S(2)}, u32[]{:S(2)}) collective-permute-start(bf16[5,1,64,256]{3,1,2,0:T(2,128)(2,1)S(1)} %get-tuple-element.77), channel_id=1, source_target_pairs={{0,4},{4,8},{8,12},{1,5},{5,9},{9,13},{2,6},{6,10},{10,14},{3,7},{... | collective-permute-start | bytes 491528 | tf_op jit(solution)/shard_map/ppermute | solution.py:23
  182.5 6.0 %collective-permute-start.10 = (bf16[5,6,1,256]{3,1,2,0:T(8,128)(2,1)S(1)}, bf16[5,6,1,256]{3,1,2,0:T(8,128)(2,1)S(1)}, u32[]{:S(2)}, u32[]{:S(2)}) collective-permute-start(bf16[5,6,1,256]{3,1,2,0:T(8,128)(2,1)S(1)} %get-tuple-element.57), channel_id=1, source_target_pairs={{0,2},{1,3},{4,6},{5,7},{8,10},{9,11},{12,14},{13,15},{16,18},{17,... | collective-permute-start | bytes 46088 | tf_op jit(solution)/shard_map/ppermute | solution.py:23
  183.8 5.7 %collective-permute-start.11 = (bf16[5,6,1,256]{3,1,2,0:T(8,128)(2,1)S(1)}, bf16[5,6,1,256]{3,1,2,0:T(8,128)(2,1)S(1)}, u32[]{:S(2)}, u32[]{:S(2)}) collective-permute-start(bf16[5,6,1,256]{3,1,2,0:T(8,128)(2,1)S(1)} %get-tuple-element.58), channel_id=1, source_target_pairs={{2,0},{3,1},{6,4},{7,5},{10,8},{11,9},{14,12},{15,13},{18,16},{19,... | collective-permute-start | bytes 46088 | tf_op jit(solution)/shard_map/ppermute | solution.py:24
where the time goes:
time: 205 us; the launch traced here: 204 us
  blocking collectives  95.1 us (46%)
  waiting for transfers between devices  28 us (14%)
  matrix products  24.9 us (12%)
  starting transfers between devices  23.2 us (11%)
  other arithmetic  18.4 us (9%)
  local copies, waits for them, and re-layouts  13 us (6%)
    psum x3, blocking collectives, activate(): lax.psum((jnp.sum(grouped, axis=(0, 2)), jnp.sum(grouped * grouped, axis=...  95.1 us
    dot_general x54, matrix products, valid_conv(): jnp.dot(window.reshape(-1, window.shape[-1]), kernel[step_t, step_y, step...  14.4 us
    ppermute x4, waiting for transfers between devices, padded_2(): after = lax.ppermute(initial, axis, down)  13.7 us
    ppermute x4, waiting for transfers between devices, passed_along(): return lax.ppermute(block, axis, route)  12 us
    ppermute x4, starting transfers between devices, padded_2(): before = lax.ppermute(last, axis, up)  11.7 us
    concatenate x6, other arithmetic, padded_2(): x = jnp.concatenate([before, x, after], axis=dim)  10.1 us
    slice x56, local copies, waits for them, and re-layouts, valid_conv(): padded[step_t:step_t + frames, step_y:step_y + height, step_x:step_x + ac...  8.07 us
    dot_general x6, matrix products, spread_taps(): jnp.dot(flattened, kernel[tap_y, tap_x], preferred_element_type=jnp.float32)  6.97 us
  transfers between devices with their start and end apart: 12, of which 10 were waited for; matrix products, arithmetic and copies ran while one was open for 4% of the time, Pallas kernels for 0%

commit v1 on v0

--- a/solution.py
+++ b/solution.py
@@ -27,6 +27,14 @@
 
 
 def activate(values, sample, scale_vec, shift_vec):
+
+    def supply_all_shelves(vec):
+        chip_axis = "ha"
+        ax_name = ("wa", "ta")
+        for q in (ax_name, chip_axis):
+            vec = lax.psum(vec, q)
+        return vec
+
     channels = values.shape[-1]
     group_width = channels // GROUPS
     grouped = sample.reshape(-1, GROUPS, group_width)
@@ -37,8 +45,8 @@
         * lax.axis_size("wa")
         * lax.axis_size("ta")
     )
-    totals, squares = lax.psum(
-        (jnp.sum(grouped, axis=(0, 2)), jnp.sum(grouped * grouped, axis=(0, 2))), ("ha", "wa", "ta")
+    totals, squares = supply_all_shelves(
+        (jnp.sum(grouped, axis=(0, 2)), jnp.sum(grouped * grouped, axis=(0, 2)))
     )
     average = totals / entries
     spread = squares / entries - average * average

time: 205 us -> 164 us (0.80)
  blocking collectives: 95.1 us -> 52.3 us
  starting transfers between devices: 23.2 us -> 25.3 us
    psum x3 -> x6, blocking collectives: 95.1 us -> 52.3 us  [supply_all_shelves(): vec = lax.psum(vec, q)]
    ppermute x4, starting transfers between devices: 11.7 us -> 14.3 us  [padded_2(): before = lax.ppermute(last, axis, up)]
  transfers between devices with their start and end apart: 12 -> 12, of which waited for: 10 -> 10; matrix products, arithmetic and copies ran while one was open for 4% -> 5% of each run, Pallas kernels for 0% -> 0%
where the time goes in v1:
time: 164 us
  blocking collectives  52.3 us (32%)
  waiting for transfers between devices  28.2 us (17%)
  starting transfers between devices  25.3 us (15%)
  matrix products  24.9 us (15%)
  other arithmetic  18.4 us (11%)
  local copies, waits for them, and re-layouts  13 us (8%)
    psum x6, blocking collectives, supply_all_shelves(): vec = lax.psum(vec, q)  52.3 us
    dot_general x54, matrix products, valid_conv(): jnp.dot(window.reshape(-1, window.shape[-1]), kernel[step_t, step_y, step...  14.4 us
    ppermute x4, starting transfers between devices, padded_2(): before = lax.ppermute(last, axis, up)  14.3 us
    ppermute x4, waiting for transfers between devices, padded_2(): after = lax.ppermute(initial, axis, down)  13.9 us
    ppermute x4, waiting for transfers between devices, passed_along(): return lax.ppermute(block, axis, route)  12 us
    concatenate x6, other arithmetic, padded_2(): x = jnp.concatenate([before, x, after], axis=dim)  10.1 us
    slice x56, local copies, waits for them, and re-layouts, valid_conv(): padded[step_t:step_t + frames, step_y:step_y + height, step_x:step_x + ac...  8.07 us
    dot_general x6, matrix products, spread_taps(): jnp.dot(flattened, kernel[tap_y, tap_x], preferred_element_type=jnp.float32)  6.98 us
  transfers between devices with their start and end apart: 12, of which 10 were waited for; matrix products, arithmetic and copies ran while one was open for 5% of the time, Pallas kernels for 0%

profile of v1, /device:TPU:0, one launch (start us, length us, event | category | flops | bytes accessed | tf_op | source)
XLA Modules:
  0.0 163.6 jit_solution(10308665977755901057)
XLA Ops:
  1.4 8.3 %all-reduce.14 = (f32[32]{0:T(128)S(1)}, f32[32]{0:T(128)S(1)}) all-reduce(f32[32]{0:T(128)S(1)} %reduce_sum.77, f32[32]{0:T(128)S(1)} %reduce_sum.74), channel_id=1, replica_groups=mesh['videos'=2,'ha'=4,'wa'=2,'ta'=2] {'wa','ta'}, use_global_device_ids=true, to_apply=%region_6.7 | all-reduce | flops 64 | bytes 512 | tf_op jit(solution)/shard_map/psum | solution.py:35
  9.7 11.9 %all-reduce.17 = (f32[32]{0:T(128)S(1)}, f32[32]{0:T(128)S(1)}) all-reduce(f32[32]{0:T(128)S(1)} %get-tuple-element.15, f32[32]{0:T(128)S(1)} %get-tuple-element.16), channel_id=1, replica_groups=mesh['videos'=2,'ha'=4,'wa'=2,'ta'=2] {'ha'}, use_global_device_ids=true, to_apply=%region_7.8 | all-reduce | flops 64 | bytes 512 | tf_op jit(solution)/shard_map/psum | solution.py:35
  38.0 6.2 %collective-permute-done = f32[3,66,256]{2,1,0:T(8,128)S(1)} collective-permute-done((f32[3,66,256]{2,1,0:T(8,128)S(1)}, f32[3,66,256]{2,1,0:T(8,128)S(1)}, u32[]{:S(2)}, u32[]{:S(2)}) %collective-permute-start) | collective-permute-done | bytes 202784 | tf_op jit(solution)/shard_map/ppermute | solution.py:13
  46.1 3.9 %collective-permute-done.1 = f32[3,4,256]{2,1,0:T(4,128)S(1)} collective-permute-done((f32[3,4,256]{2,1,0:T(4,128)S(1)}, f32[3,4,256]{2,1,0:T(4,128)S(1)}, u32[]{:S(2)}, u32[]{:S(2)}) %collective-permute-start.1) | collective-permute-done | bytes 12320 | tf_op jit(solution)/shard_map/ppermute | solution.py:13
  50.9 5.8 %all-reduce.13 = (f32[32]{0:T(128)S(1)}, f32[32]{0:T(128)S(1)}) all-reduce(f32[32]{0:T(128)S(1)} %reduce_sum.89, f32[32]{0:T(128)S(1)} %reduce_sum.83), channel_id=1, replica_groups=mesh['videos'=2,'ha'=4,'wa'=2,'ta'=2] {'wa','ta'}, use_global_device_ids=true, to_apply=%region_14.15 | all-reduce | flops 64 | bytes 512 | tf_op jit(solution)/shard_map/psum | solution.py:35
  56.6 8.4 %all-reduce.16 = (f32[32]{0:T(128)S(1)}, f32[32]{0:T(128)S(1)}) all-reduce(f32[32]{0:T(128)S(1)} %get-tuple-element.13, f32[32]{0:T(128)S(1)} %get-tuple-element.14), channel_id=1, replica_groups=mesh['videos'=2,'ha'=4,'wa'=2,'ta'=2] {'ha'}, use_global_device_ids=true, to_apply=%region_15.16 | all-reduce | flops 64 | bytes 512 | tf_op jit(solution)/shard_map/psum | solution.py:35
  66.1 1.3 collective-permute-start.2
  70.8 4.6 %collective-permute-start.3 = (bf16[5,1,64,256]{3,1,2,0:T(2,128)(2,1)S(1)}, bf16[5,1,64,256]{3,1,2,0:T(2,128)(2,1)S(1)}, u32[]{:S(2)}, u32[]{:S(2)}) collective-permute-start(bf16[5,1,64,256]{3,1,2,0:T(2,128)(2,1)S(1)} %get-tuple-element.87), channel_id=1, source_target_pairs={{0,4},{4,8},{8,12},{1,5},{5,9},{9,13},{2,6},{6,10},{10,14},{3,7},{... | collective-permute-start | bytes 491528 | tf_op jit(solution)/shard_map/ppermute | solution.py:23
  75.5 6.2 %collective-permute-done.4 = bf16[5,1,64,256]{3,1,2,0:T(2,128)(2,1)S(1)} collective-permute-done((bf16[5,1,64,256]{3,1,2,0:T(2,128)(2,1)S(1)}, bf16[5,1,64,256]{3,1,2,0:T(2,128)(2,1)S(1)}, u32[]{:S(2)}, u32[]{:S(2)}) %collective-permute-start.4) | collective-permute-done | bytes 163872 | tf_op jit(solution)/shard_map/ppermute | solution.py:24
  82.9 1.7 %collective-permute-start.5 = (bf16[5,6,1,256]{3,1,2,0:T(8,128)(2,1)S(1)}, bf16[5,6,1,256]{3,1,2,0:T(8,128)(2,1)S(1)}, u32[]{:S(2)}, u32[]{:S(2)}) collective-permute-start(bf16[5,6,1,256]{3,1,2,0:T(8,128)(2,1)S(1)} %get-tuple-element.67), channel_id=1, source_target_pairs={{0,2},{1,3},{4,6},{5,7},{8,10},{9,11},{12,14},{13,15},{16,18},{17,... | collective-permute-start | bytes 46088 | tf_op jit(solution)/shard_map/ppermute | solution.py:23
  84.6 1.5 collective-permute-start.6
  87.4 1.7 %pad_maximum_fusion.15 = (bf16[3,4,64,256]{3,1,2,0:T(4,128)(2,1)S(1)}, bf16[3,4,64,256]{3,1,2,0:T(4,128)(2,1)S(1)}, bf16[3,4,64,256]{3,1,2,0:T(4,128)(2,1)S(1)},...) fusion(bf16[5,1,64,256]{3,1,2,0:T(2,128)(2,1)S(1)} %collective-permute-done.4, ...), kind=kLoop, calls=%fused_computation.128 | loop fusion | flops 5111808 | bytes 2785280 | tf_op jit(solution)/shard_map/concatenate | solution.py:25
  90.3 2.3 %maximum_maximum_fusion = (bf16[5,6,65,256]{3,1,2,0:T(8,128)(2,1)S(1)}, bf16[5,6,65,256]{3,1,2,0:T(8,128)(2,1)S(1)}) fusion(bf16[5,1,64,256]{3,1,2,0:T(2,128)(2,1)S(1)} %collective-permute-done.4, bf16[3,4,64,256]{3,1,2,0:T(4,128)(2,1)S(1)} %fusion.13, bf16[2,4,64,256]{3,1,2,0:T(4,128)(2,1)S(1)} %maximum_select_fusion, ...), kind=kLoop, calls=%fused_computation.5 | loop fusion | flops 9984000 | bytes 3010560 | tf_op jit(solution)/shard_map/concatenate | solution.py:25
  92.6 1.6 fusion.182
  94.2 1.3 fusion.183
  103.9 6.1 %all-reduce.12 = (f32[32]{0:T(128)S(1)}, f32[32]{0:T(128)S(1)}) all-reduce(f32[32]{0:T(128)S(1)} %reduce_sum.113, f32[32]{0:T(128)S(1)} %reduce_sum.110), channel_id=1, replica_groups=mesh['videos'=2,'ha'=4,'wa'=2,'ta'=2] {'wa','ta'}, use_global_device_ids=true, to_apply=%region_22.23 | all-reduce | flops 64 | bytes 512 | tf_op jit(solution)/shard_map/psum | solution.py:35
  110.0 11.8 %all-reduce.15 = (f32[32]{0:T(128)S(1)}, f32[32]{0:T(128)S(1)}) all-reduce(f32[32]{0:T(128)S(1)} %get-tuple-element.11, f32[32]{0:T(128)S(1)} %get-tuple-element.12), channel_id=1, replica_groups=mesh['videos'=2,'ha'=4,'wa'=2,'ta'=2] {'ha'}, use_global_device_ids=true, to_apply=%region_23.24 | all-reduce | flops 64 | bytes 512 | tf_op jit(solution)/shard_map/psum | solution.py:35
  123.0 1.8 %collective-permute-start.7 = (bf16[2,4,64,256]{3,1,2,0:T(4,128)(2,1)S(1)}, bf16[2,4,64,256]{3,1,2,0:T(4,128)(2,1)S(1)}, u32[]{:S(2)}, u32[]{:S(2)}) collective-permute-start(bf16[2,4,64,256]{3,1,2,0:T(4,128)(2,1)S(1)} %slice.620), channel_id=1, source_target_pairs={{0,1},{2,3},{4,5},{6,7},{8,9},{10,11},{12,13},{14,15},{16,17},{18,... | collective-permute-start | bytes 786440 | tf_op jit(solution)/shard_map/ppermute | solution.py:13
  128.0 4.6 %collective-permute-start.8 = (bf16[5,1,64,256]{3,1,2,0:T(2,128)(2,1)S(1)}, bf16[5,1,64,256]{3,1,2,0:T(2,128)(2,1)S(1)}, u32[]{:S(2)}, u32[]{:S(2)}) collective-permute-start(bf16[5,1,64,256]{3,1,2,0:T(2,128)(2,1)S(1)} %get-tuple-element.83), channel_id=1, source_target_pairs={{0,4},{4,8},{8,12},{1,5},{5,9},{9,13},{2,6},{6,10},{10,14},{3,7},{... | collective-permute-start | bytes 491528 | tf_op jit(solution)/shard_map/ppermute | solution.py:23
  132.6 6.0 %collective-permute-done.9 = bf16[5,1,64,256]{3,1,2,0:T(2,128)(2,1)S(1)} collective-permute-done((bf16[5,1,64,256]{3,1,2,0:T(2,128)(2,1)S(1)}, bf16[5,1,64,256]{3,1,2,0:T(2,128)(2,1)S(1)}, u32[]{:S(2)}, u32[]{:S(2)}) %collective-permute-start.9) | collective-permute-done | bytes 163872 | tf_op jit(solution)/shard_map/ppermute | solution.py:24
  139.8 3.4 %collective-permute-start.10 = (bf16[5,6,1,256]{3,1,2,0:T(8,128)(2,1)S(1)}, bf16[5,6,1,256]{3,1,2,0:T(8,128)(2,1)S(1)}, u32[]{:S(2)}, u32[]{:S(2)}) collective-permute-start(bf16[5,6,1,256]{3,1,2,0:T(8,128)(2,1)S(1)} %get-tuple-element.63), channel_id=1, source_target_pairs={{0,2},{1,3},{4,6},{5,7},{8,10},{9,11},{12,14},{13,15},{16,18},{17,... | collective-permute-start | bytes 46088 | tf_op jit(solution)/shard_map/ppermute | solution.py:23
  145.8 1.7 %pad_maximum_fusion.6 = (bf16[3,4,64,256]{3,1,2,0:T(4,128)(2,1)S(1)}, bf16[3,4,64,256]{3,1,2,0:T(4,128)(2,1)S(1)}, bf16[3,4,64,256]{3,1,2,0:T(4,128)(2,1)S(1)}, ...) fusion(bf16[5,1,64,256]{3,1,2,0:T(2,128)(2,1)S(1)} %collective-permute-done.9, ...), kind=kLoop, calls=%fused_computation.119 | loop fusion | flops 5111808 | bytes 2785280 | tf_op jit(solution)/shard_map/concatenate | solution.py:25
  148.9 2.3 %maximum_maximum_fusion.1 = (bf16[5,6,65,256]{3,1,2,0:T(8,128)(2,1)S(1)}, bf16[5,6,65,256]{3,1,2,0:T(8,128)(2,1)S(1)}) fusion(bf16[5,1,64,256]{3,1,2,0:T(2,128)(2,1)S(1)} %collective-permute-done.9, bf16[3,4,64,256]{3,1,2,0:T(4,128)(2,1)S(1)} %fusion.14, bf16[2,4,64,256]{3,1,2,0:T(4,128)(2,1)S(1)} %maximum_select_fusion.1, ...), kind=kLoop, calls=%fused_computation.7 | loop fusion | flops 9984000 | bytes 3010560 | tf_op jit(solution)/shard_map/concatenate | solution.py:25
  151.3 1.6 fusion.180
  (208 shorter events, 56.2 us)
Async XLA Ops:
  36.3 29.1 %copy-start.2 = (f32[256]{0:T(256)S(1)}, f32[256]{0:T(256)}, u32[]{:S(2)}) copy-start(f32[256]{0:T(256)} %param.15) | copy-start | bytes 3076
  36.3 29.1 %copy-start.3 = (f32[256]{0:T(256)S(1)}, f32[256]{0:T(256)}, u32[]{:S(2)}) copy-start(f32[256]{0:T(256)} %param.14) | copy-start | bytes 3076
  36.3 7.8 %collective-permute-start = (f32[3,66,256]{2,1,0:T(8,128)S(1)}, f32[3,66,256]{2,1,0:T(8,128)S(1)}, u32[]{:S(2)}, u32[]{:S(2)}) collective-permute-start(f32[3,66,256]{2,1,0:T(8,128)S(1)} %get-tuple-element.59), channel_id=1, source_target_pairs={{4,0},{8,4},{12,8},{5,1},{9,5},{13,9},{6,2},{10,6},{14,10},{7,3},{... | collective-permute-start | bytes 608264 | tf_op jit(solution)/shard_map/ppermute | solution.py:13
  44.4 5.6 %collective-permute-start.1 = (f32[3,4,256]{2,1,0:T(4,128)S(1)}, f32[3,4,256]{2,1,0:T(4,128)S(1)}, u32[]{:S(2)}, u32[]{:S(2)}) collective-permute-start(f32[3,4,256]{2,1,0:T(4,128)S(1)} %fusion.176), channel_id=1, source_target_pairs={{2,0},{3,1},{6,4},{7,5},{10,8},{11,9},{14,12},{15,13},{18,16},{19,... | collective-permute-start | bytes 36872 | tf_op jit(solution)/shard_map/ppermute | solution.py:13
  66.1 2.4 %collective-permute-start.2 = (bf16[2,4,64,256]{3,1,2,0:T(4,128)(2,1)S(1)}, bf16[2,4,64,256]{3,1,2,0:T(4,128)(2,1)S(1)}, u32[]{:S(2)}, u32[]{:S(2)}) collective-permute-start(bf16[2,4,64,256]{3,1,2,0:T(4,128)(2,1)S(1)} %slice.594), channel_id=1, source_target_pairs={{0,1},{2,3},{4,5},{6,7},{8,9},{10,11},{12,13},{14,15},{16,17},{18,... | collective-permute-start | bytes 786440 | tf_op jit(solution)/shard_map/ppermute | solution.py:13
  67.4 19.6 %copy-start = (bf16[3,3,3,256,256]{4,3,2,1,0:T(8,128)(2,1)S(1)}, bf16[3,3,3,256,256]{4,3,2,1,0:T(8,128)(2,1)}, u32[]{:S(2)}) copy-start(bf16[3,3,3,256,256]{4,3,2,1,0:T(8,128)(2,1)} %param.16) | copy-start | bytes 10616836
  69.5 12.1 %collective-permute-start.4 = (bf16[5,1,64,256]{3,1,2,0:T(2,128)(2,1)S(1)}, bf16[5,1,64,256]{3,1,2,0:T(2,128)(2,1)S(1)}, u32[]{:S(2)}, u32[]{:S(2)}) collective-permute-start(bf16[5,1,64,256]{3,1,2,0:T(2,128)(2,1)S(1)} %get-tuple-element.88), channel_id=1, source_target_pairs={{4,0},{8,4},{12,8},{5,1},{9,5},{13,9},{6,2},{10,6},{14,10},{7,3},{... | collective-permute-start | bytes 491528 | tf_op jit(solution)/shard_map/ppermute | solution.py:24
  70.8 12.0 %collective-permute-start.3 = (bf16[5,1,64,256]{3,1,2,0:T(2,128)(2,1)S(1)}, bf16[5,1,64,256]{3,1,2,0:T(2,128)(2,1)S(1)}, u32[]{:S(2)}, u32[]{:S(2)}) collective-permute-start(bf16[5,1,64,256]{3,1,2,0:T(2,128)(2,1)S(1)} %get-tuple-element.87), channel_id=1, source_target_pairs={{0,4},{4,8},{8,12},{1,5},{5,9},{9,13},{2,6},{6,10},{10,14},{3,7},{... | collective-permute-start | bytes 491528 | tf_op jit(solution)/shard_map/ppermute | solution.py:23
  82.9 6.6 %collective-permute-start.5 = (bf16[5,6,1,256]{3,1,2,0:T(8,128)(2,1)S(1)}, bf16[5,6,1,256]{3,1,2,0:T(8,128)(2,1)S(1)}, u32[]{:S(2)}, u32[]{:S(2)}) collective-permute-start(bf16[5,6,1,256]{3,1,2,0:T(8,128)(2,1)S(1)} %get-tuple-element.67), channel_id=1, source_target_pairs={{0,2},{1,3},{4,6},{5,7},{8,10},{9,11},{12,14},{13,15},{16,18},{17,... | collective-permute-start | bytes 46088 | tf_op jit(solution)/shard_map/ppermute | solution.py:23
  84.6 5.7 %collective-permute-start.6 = (bf16[5,6,1,256]{3,1,2,0:T(8,128)(2,1)S(1)}, bf16[5,6,1,256]{3,1,2,0:T(8,128)(2,1)S(1)}, u32[]{:S(2)}, u32[]{:S(2)}) collective-permute-start(bf16[5,6,1,256]{3,1,2,0:T(8,128)(2,1)S(1)} %get-tuple-element.68), channel_id=1, source_target_pairs={{2,0},{3,1},{6,4},{7,5},{10,8},{11,9},{14,12},{15,13},{18,16},{19,... | collective-permute-start | bytes 46088 | tf_op jit(solution)/shard_map/ppermute | solution.py:24
  102.6 19.5 %copy-start.4 = (f32[256]{0:T(256)S(1)}, f32[256]{0:T(256)}, u32[]{:S(2)}) copy-start(f32[256]{0:T(256)} %param.18) | copy-start | bytes 3076
  102.6 19.5 %copy-start.5 = (f32[256]{0:T(256)S(1)}, f32[256]{0:T(256)}, u32[]{:S(2)}) copy-start(f32[256]{0:T(256)} %param.17) | copy-start | bytes 3076
  122.9 22.7 %copy-start.1 = (bf16[3,3,3,256,256]{4,3,2,1,0:T(8,128)(2,1)S(1)}, bf16[3,3,3,256,256]{4,3,2,1,0:T(8,128)(2,1)}, u32[]{:S(2)}) copy-start(bf16[3,3,3,256,256]{4,3,2,1,0:T(8,128)(2,1)} %param.19) | copy-start | bytes 10616836
  123.0 2.7 %collective-permute-start.7 = (bf16[2,4,64,256]{3,1,2,0:T(4,128)(2,1)S(1)}, bf16[2,4,64,256]{3,1,2,0:T(4,128)(2,1)S(1)}, u32[]{:S(2)}, u32[]{:S(2)}) collective-permute-start(bf16[2,4,64,256]{3,1,2,0:T(4,128)(2,1)S(1)} %slice.620), channel_id=1, source_target_pairs={{0,1},{2,3},{4,5},{6,7},{8,9},{10,11},{12,13},{14,15},{16,17},{18,... | collective-permute-start | bytes 786440 | tf_op jit(solution)/shard_map/ppermute | solution.py:13
  126.7 11.9 %collective-permute-start.9 = (bf16[5,1,64,256]{3,1,2,0:T(2,128)(2,1)S(1)}, bf16[5,1,64,256]{3,1,2,0:T(2,128)(2,1)S(1)}, u32[]{:S(2)}, u32[]{:S(2)}) collective-permute-start(bf16[5,1,64,256]{3,1,2,0:T(2,128)(2,1)S(1)} %get-tuple-element.84), channel_id=1, source_target_pairs={{4,0},{8,4},{12,8},{5,1},{9,5},{13,9},{6,2},{10,6},{14,10},{7,3},{... | collective-permute-start | bytes 491528 | tf_op jit(solution)/shard_map/ppermute | solution.py:24
  128.0 11.8 %collective-permute-start.8 = (bf16[5,1,64,256]{3,1,2,0:T(2,128)(2,1)S(1)}, bf16[5,1,64,256]{3,1,2,0:T(2,128)(2,1)S(1)}, u32[]{:S(2)}, u32[]{:S(2)}) collective-permute-start(bf16[5,1,64,256]{3,1,2,0:T(2,128)(2,1)S(1)} %get-tuple-element.83), channel_id=1, source_target_pairs={{0,4},{4,8},{8,12},{1,5},{5,9},{9,13},{2,6},{6,10},{10,14},{3,7},{... | collective-permute-start | bytes 491528 | tf_op jit(solution)/shard_map/ppermute | solution.py:23
  139.8 8.2 %collective-permute-start.10 = (bf16[5,6,1,256]{3,1,2,0:T(8,128)(2,1)S(1)}, bf16[5,6,1,256]{3,1,2,0:T(8,128)(2,1)S(1)}, u32[]{:S(2)}, u32[]{:S(2)}) collective-permute-start(bf16[5,6,1,256]{3,1,2,0:T(8,128)(2,1)S(1)} %get-tuple-element.63), channel_id=1, source_target_pairs={{0,2},{1,3},{4,6},{5,7},{8,10},{9,11},{12,14},{13,15},{16,18},{17,... | collective-permute-start | bytes 46088 | tf_op jit(solution)/shard_map/ppermute | solution.py:23
  143.2 5.7 %collective-permute-start.11 = (bf16[5,6,1,256]{3,1,2,0:T(8,128)(2,1)S(1)}, bf16[5,6,1,256]{3,1,2,0:T(8,128)(2,1)S(1)}, u32[]{:S(2)}, u32[]{:S(2)}) collective-permute-start(bf16[5,6,1,256]{3,1,2,0:T(8,128)(2,1)S(1)} %get-tuple-element.64), channel_id=1, source_target_pairs={{2,0},{3,1},{6,4},{7,5},{10,8},{11,9},{14,12},{15,13},{18,16},{19,... | collective-permute-start | bytes 46088 | tf_op jit(solution)/shard_map/ppermute | solution.py:24
